TPU v7x, 32 devices: a whole 2x2x4 slice. The times are simulated.
32 devices in a mesh: groups: 2 (over y), picks: 4 (over z), heads: 4 (over x, core).
Axes of the slice: x: 2, y: 2, z: 4, core: 2. Of those that a mesh axis runs over, the one named last changes fastest.
Arguments:
- coords: float32 [3, 8192], P(None, ('groups', 'picks')), parts along dimension 1, may hold values from -1 to 1
- horizon_ids: int32 [8192], P(('groups', 'picks')), parts along dimension 0, may hold values from 0 to 63
- horizon_levels: float32 [128], P('groups'), parts along dimension 0, may hold values from -2 to 2
- latents: bfloat16 [512, 1024], replicated, may hold values from -960 to 960
- kv_weight: bfloat16 [3072, 2, 1024], P('picks', None, 'heads'), may hold values from -0.109375 to 0.109375
- cross_out: bfloat16 [1024, 1024], P('heads'), may hold values from -0.75 to 0.75
- norm_gains: float32 [2, 1024], replicated, may hold values from 0.1 to 1.9
- self_qkv: bfloat16 [3, 1024, 1024], P(None, None, 'heads'), may hold values from -0.1875 to 0.1875
- self_out: bfloat16 [1024, 1024], P(None, 'heads'), may hold values from -0.1875 to 0.1875
- dec_kv: bfloat16 [2, 1024, 1024], P(None, None, 'heads'), may hold values from -0.1875 to 0.1875
- dec_query: bfloat16 [3072, 1024], P('picks', 'heads'), may hold values from -0.109375 to 0.109375
- readout: float32 [1024], P('heads'), may hold values from -0.1875 to 0.1875
Outputs:
- field: float32 [8192], P(('groups', 'picks')), parts along dimension 0
- latents_out: float32 [1024, 1024], P('groups', 'heads'), parts along dimension 0
- grad_query: float32 [6144, 1024], P(('groups', 'picks'), 'heads'), parts along dimension 0
There are 2 independent parts, one for each index of `groups`. A program takes and returns all parts, laid end to end along the dimension named above; an argument that names none is the same for every part. Nothing has to cross between parts.
All inputs are finite; a program needn't handle non-finite values.
Results may differ from a plain program's by a relative error of at most 0.028.
Values may be sent and summed in bfloat16 or wider, within the bound.
No kernel may reach another device: no remote copies, remote signals or barrier semaphores. Data moves between devices by JAX's collectives and lax.ppermute only.
A program may use at most 64 MiB of HBM per device.

v0:
```python
import functools
import jax
import jax.numpy as jnp
from jax import lax
from jax.sharding import PartitionSpec as P

HEAD = 128
BANDS = 512
HORIZONS = 64
PI = 3.141592653589793
EPS = 1e-06
RING_MAX = 4


def encode(coords):
    freq = jnp.linspace(1.0, BANDS / 2.0, BANDS).astype(jnp.float32)
    angle = PI * freq[None, :, None] * coords[:, None, :]
    table = jnp.concatenate([jnp.sin(angle), jnp.cos(angle)], axis=0)
    return table.reshape(6 * BANDS, coords.shape[1]).T.astype(jnp.bfloat16)


def ring_gather(x, axis, n):
    if n == 1:
        return x
    if n > RING_MAX:
        return lax.all_gather(x, axis, axis=0, tiled=True)
    idx = lax.axis_index(axis)
    blocks = [x]
    for s in range(1, n):
        blocks.append(lax.ppermute(x, axis, [(i, (i - s) % n) for i in range(n)]))
    flipped = jnp.stack(blocks)
    ordered = jnp.roll(flipped, idx, axis=0)
    return ordered.reshape((n * x.shape[0],) + x.shape[1:])


def on_device(
    coords,
    horizon_ids,
    horizon_levels,
    latents,
    kv_weight,
    cross_out,
    norm_gains,
    self_qkv,
    self_out,
    dec_kv,
    dec_query,
    readout,
    *,
    n_picks,
    n_heads
):
    high = lax.Precision.HIGHEST
    scale = HEAD ** (-0.5)
    count = coords.shape[1]
    width = latents.shape[1]
    lat_rows = latents.shape[0]
    local = kv_weight.shape[2]
    nheads = local // HEAD
    column = lax.axis_index("heads") * local
    enc = encode(coords)
    cross_full = ring_gather(cross_out, "heads", n_heads)
    piece = lax.all_gather(kv_weight, "picks", axis=0, tiled=True)
    keys_vals = jnp.dot(
        enc, piece.reshape(piece.shape[0], 2 * local), preferred_element_type=jnp.float32
    ).astype(jnp.bfloat16)
    keys = keys_vals[:, :local].reshape(count, nheads, HEAD)
    values = keys_vals[:, local:].reshape(count, nheads, HEAD)
    queries = lax.dynamic_slice_in_dim(latents, column, local, 1).reshape(lat_rows, nheads, HEAD)
    scores = jnp.einsum("lhc,thc->hlt", queries, keys, preferred_element_type=jnp.float32) * scale
    top = jnp.max(scores, axis=2)
    expo = jnp.exp(scores - top[:, :, None])
    total = jnp.sum(expo, axis=2)
    numer = jnp.einsum(
        "hlt,thc->hlc", expo.astype(jnp.bfloat16), values, preferred_element_type=jnp.float32
    )
    all_numer = lax.all_gather(numer.astype(jnp.bfloat16), "picks", axis=0, tiled=False)
    all_stats = lax.all_gather(jnp.stack([top, total]), "picks", axis=0, tiled=False)
    best = jnp.max(all_stats[:, 0], axis=0)
    factor = jnp.exp(all_stats[:, 0] - best[None])
    merged_total = jnp.sum(factor * all_stats[:, 1], axis=0)
    merged_numer = jnp.einsum(
        "phl,phlc->hlc", factor, all_numer.astype(jnp.float32), precision=high
    )
    attended = (
        (merged_numer / merged_total[:, :, None])
        .transpose(1, 0, 2)
        .reshape(lat_rows, local)
        .astype(jnp.bfloat16)
    )
    dq_local, attended = lax.optimization_barrier((dec_query, attended))
    dq_full = ring_gather(dq_local, "picks", n_picks)
    gain_two = lax.dynamic_slice_in_dim(norm_gains[1], column, local, 0)
    attended_full = lax.all_gather(attended, "heads", axis=1, tiled=True)
    whole = latents.astype(jnp.float32) + jnp.dot(
        attended_full, cross_full, preferred_element_type=jnp.float32
    )
    power = jnp.mean(whole * whole, axis=1, keepdims=True)
    normed = (whole * lax.rsqrt(power + EPS) * norm_gains[0][None, :]).astype(jnp.bfloat16)
    state = lax.dynamic_slice_in_dim(whole, column, local, 1)
    qkv = jnp.einsum("ld,kde->kle", normed, self_qkv, preferred_element_type=jnp.float32).astype(
        jnp.bfloat16
    )
    self_q = qkv[0].reshape(lat_rows, nheads, HEAD)
    self_k = qkv[1].reshape(lat_rows, nheads, HEAD)
    self_v = qkv[2].reshape(lat_rows, nheads, HEAD)
    inner = jnp.einsum("lhc,mhc->hlm", self_q, self_k, preferred_element_type=jnp.float32) * scale
    raised = jnp.exp(inner)
    probs = (raised / jnp.sum(raised, axis=2, keepdims=True)).astype(jnp.bfloat16)
    head_out = (
        jnp.einsum("hlm,mhc->lhc", probs, self_v, preferred_element_type=jnp.float32)
        .astype(jnp.bfloat16)
        .reshape(lat_rows, local)
    )
    every_head = lax.all_gather(head_out, "heads", axis=1, tiled=True)
    latents_out = state + jnp.dot(every_head, self_out, preferred_element_type=jnp.float32)
    gained = (latents_out * gain_two[None, :]).astype(jnp.bfloat16)
    gained_full = lax.all_gather(gained, "heads", axis=1, tiled=True)
    power_two = lax.psum(jnp.sum(latents_out * latents_out, axis=1), "heads")
    row_scale = lax.rsqrt(power_two / width + EPS)
    dec = (
        jnp.einsum("ld,kde->kle", gained_full, dec_kv, preferred_element_type=jnp.float32)
        * row_scale[None, :, None]
    ).astype(jnp.bfloat16)
    dec_keys = dec[0].reshape(lat_rows, nheads, HEAD)
    dec_vals = dec[1].reshape(lat_rows, nheads, HEAD)
    query = jnp.dot(enc, dq_full, preferred_element_type=jnp.float32).astype(jnp.bfloat16)
    dec_q = query.reshape(count, nheads, HEAD)
    logits = jnp.einsum("thc,lhc->htl", dec_q, dec_keys, preferred_element_type=jnp.float32) * scale
    lifted = jnp.exp(logits)
    weights = lifted / jnp.sum(lifted, axis=2, keepdims=True)
    out = jnp.einsum(
        "htl,lhc->thc", weights.astype(jnp.bfloat16), dec_vals, preferred_element_type=jnp.float32
    )
    read = readout.reshape(nheads, HEAD)
    field = lax.psum(jnp.sum(out * read[None, :, :], axis=(1, 2)), "heads")
    onehot = (horizon_ids[:, None] == jnp.arange(HORIZONS, dtype=jnp.int32)[None, :]).astype(
        jnp.float32
    )
    target = jnp.sum(onehot * horizon_levels[None, :], axis=1)
    miss = field - target
    value_read = jnp.einsum("lhc,hc->hl", dec_vals.astype(jnp.float32), read, precision=high)
    dprob = miss[None, :, None] * value_read[:, None, :]
    dscore = (weights * (dprob - jnp.sum(dprob * weights, axis=2, keepdims=True))).astype(
        jnp.bfloat16
    )
    dquery = (
        (jnp.einsum("htl,lhc->thc", dscore, dec_keys, preferred_element_type=jnp.float32) * scale)
        .reshape(count, local)
        .astype(jnp.bfloat16)
    )
    grad_query = lax.psum_scatter(
        jnp.dot(enc.T, dquery, preferred_element_type=jnp.float32).astype(jnp.bfloat16),
        "picks",
        scatter_dimension=0,
        tiled=True,
    ).astype(jnp.float32)
    return (field, latents_out, grad_query)


def solution(mesh):
    in_specs = (
        P(None, ("groups", "picks")),
        P(("groups", "picks")),
        P("groups"),
        P(),
        P("picks", None, "heads"),
        P("heads", None),
        P(),
        P(None, None, "heads"),
        P(None, "heads"),
        P(None, None, "heads"),
        P("picks", "heads"),
        P("heads"),
    )
    out_specs = (P(("groups", "picks")), P("groups", "heads"), P(("groups", "picks"), "heads"))
    body = functools.partial(on_device, n_picks=mesh.shape["picks"], n_heads=mesh.shape["heads"])
    return jax.shard_map(body, mesh=mesh, in_specs=in_specs, out_specs=out_specs, check_vma=False)
```

profile of v0, /device:TPU:0, one launch (start us, length us, event | category | flops | bytes accessed | tf_op | source)
XLA Modules:
  0.0 272.0 jit_solution(7602422129302060528)
XLA Ops:
  9.2 23.6 %fusion = (bf16[3,512,1024]{2,1,0:T(8,128)(2,1)S(1)}, bf16[3,512,1024]{2,1,0:T(8,128)(2,1)S(1)}) fusion(f32[3,1024]{1,0:T(4,128)} %param.12, f32[512]{0:T(512)S(1)} %maximum_multiply_fusion), kind=kLoop, calls=%fused_computation.2 | loop fusion | flops 4718592 | bytes 6305792 | tf_op jit(solution)/shard_map/convert
  32.8 3.2 %pad_maximum_fusion = bf16[6,512,1024]{2,1,0:T(8,128)(2,1)} fusion(bf16[3,512,1024]{2,1,0:T(8,128)(2,1)S(1)} %get-tuple-element.19, bf16[3,512,1024]{2,1,0:T(8,128)(2,1)S(1)} %get-tuple-element.18), kind=kLoop, calls=%fused_computation.4 | loop fusion | flops 3145728 | bytes 12582912 | tf_op jit(solution)/shard_map/concatenate | solution.py:18
  36.0 39.9 %all-gather.8.cloned.1.call-done = bf16[3072,2,256]{2,1,0:T(2,128)(2,1)} async-done(((bf16[768,2,256]{2,1,0:T(2,128)(2,1)}), bf16[3072,2,256]{2,1,0:T(2,128)(2,1)}) %all-gather.8.cloned.1.call-update) | async-done | bytes 3145744 | tf_op jit(solution)/shard_map/all_gather | solution.py:63
  75.8 2.6 copy.98
  79.6 3.5 %convolution_convert_fusion.1 = bf16[1024,512]{0,1:T(8,128)(2,1)S(1)} fusion(bf16[3072,1024]{1,0:T(8,128)(2,1)S(1)} %bitcast.122, bf16[3072,512]{1,0:T(8,128)(2,1)S(1)} %bitcast.127), kind=kOutput, calls=%fused_computation.33 | convolution fusion | flops 3221749760 | bytes 10485760 | tf_op jit(solution)/shard_map/dot_general | solution.py:64
  84.1 2.0 copy-done.2
  90.4 10.5 %collective-permute-done = bf16[256,1024]{1,0:T(8,128)(2,1)S(1)} collective-permute-done((bf16[256,1024]{1,0:T(8,128)(2,1)S(1)}, bf16[256,1024]{1,0:T(8,128)(2,1)S(1)}, u32[]{:S(2)}, u32[]{:S(2)}) %collective-permute-start) | collective-permute-done | bytes 524320 | tf_op jit(solution)/shard_map/ppermute | solution.py:30
  101.7 3.1 %fusion.7 = f32[2,512]{1,0:T(2,128)S(1)} fusion(f32[2,512,1024]{2,1,0:T(8,128)} %copy-done.2, f32[2,512]{1,0:T(2,128)S(1)} %get-tuple-element.22), kind=kLoop, calls=%fused_computation.16 | loop fusion | flops 3144704 | bytes 4202496 | tf_op jit(solution)/shard_map/reduce_sum | solution.py:73
  104.8 13.3 %all-gather.1 = f32[8,2,512]{2,1,0:T(2,128)S(1)} all-gather(f32[2,2,512]{2,1,0:T(2,128)S(1)} %pad_maximum_fusion.1), channel_id=3, replica_groups=mesh['groups'=2,'picks'=4,'heads'=4] {'picks'}, dimensions={0}, use_global_device_ids=true | all-gather | bytes 40960 | tf_op jit(solution)/shard_map/all_gather | solution.py:78
  119.3 5.3 %fusion.44 = f32[512,2,1,128]{3,2,1,0:T(1,128)S(1)} fusion(f32[4,2,512,1]{0,3,1,2:T(1,128)} %copy.81, bf16[4,2,512,128]{3,2,1,0:T(8,128)(2,1)} %bitcast.156), kind=kOutput, calls=%fused_computation.51 | convolution fusion | flops 6291456 | bytes 1589248 | tf_op jit(solution)/shard_map/phl,phlc->hlc/dot_general | solution.py:82
  133.3 3.1 %constant_dynamic-slice_fusion.2 = bf16[4,256,1024]{2,1,0:T(8,128)(2,1)} fusion(bf16[8,256,1024]{2,1,0:T(8,128)(2,1)} %bitcast_dynamic-update-slice_fusion.1, s32[]{:T(128)S(6)} %select_n.30), kind=kLoop, calls=%fused_computation.93 | loop fusion | bytes 4194308 | tf_op jit(solution)/shard_map/jit(_roll_dynamic)/dynamic_slice | solution.py:32
  136.4 4.8 %all-gather.10.cloned.1.call-done = bf16[512,1024]{1,0:T(8,128)(2,1)} async-done(((bf16[512,256]{1,0:T(8,128)(2,1)}), bf16[512,1024]{1,0:T(8,128)(2,1)}) %all-gather.10.cloned.1.call-update) | async-done | bytes 1048592 | tf_op jit(solution)/shard_map/all_gather | solution.py:94
  141.2 3.5 %multiply_reduce_fusion.1 = (f32[512]{0:T(512)S(1)}, f32[512,1024]{1,0:T(8,128)S(1)}) fusion(bf16[512,1024]{1,0:T(8,128)(2,1)} %all-gather.10.cloned.1.call-done, bf16[1024,1024]{1,0:T(8,128)(2,1)} %bitcast.128, bf16[512,1024]{1,0:T(8,128)(2,1)} %param.15), kind=kOutput, calls=%fused_computation.28 | convolution fusion | flops 1075838464 | bytes 6293504 | tf_op jit(solution)/shard_map/dot_general | solution.py:95
  147.8 3.4 %collective-permute-start.3 = (bf16[768,256]{1,0:T(8,128)(2,1)S(1)}, bf16[768,256]{1,0:T(8,128)(2,1)S(1)}, u32[]{:S(2)}, u32[]{:S(2)}) collective-permute-start(bf16[768,256]{1,0:T(8,128)(2,1)S(1)} %copy-done.7), channel_id=1, source_target_pairs={{0,12},{4,0},{8,4},{12,8},{1,13},{5,1},{9,5},{13,9},{2,14},{6,2},{... | collective-permute-start | bytes 1179656 | tf_op jit(solution)/shard_map/ppermute | solution.py:30
  153.3 7.5 %collective-permute-done.3 = bf16[768,256]{1,0:T(8,128)(2,1)S(1)} collective-permute-done((bf16[768,256]{1,0:T(8,128)(2,1)S(1)}, bf16[768,256]{1,0:T(8,128)(2,1)S(1)}, u32[]{:S(2)}, u32[]{:S(2)}) %collective-permute-start.3) | collective-permute-done | bytes 393248 | tf_op jit(solution)/shard_map/ppermute | solution.py:30
  161.5 23.8 %collective-permute-done.4 = bf16[768,256]{1,0:T(8,128)(2,1)S(1)} collective-permute-done((bf16[768,256]{1,0:T(8,128)(2,1)S(1)}, bf16[768,256]{1,0:T(8,128)(2,1)S(1)}, u32[]{:S(2)}, u32[]{:S(2)}) %collective-permute-start.4) | collective-permute-done | bytes 393248 | tf_op jit(solution)/shard_map/ppermute | solution.py:30
  187.7 2.7 multiply_reduce_fusion.2
  194.5 5.0 %convolution_convert_fusion.3 = bf16[1024,256]{0,1:T(8,128)(2,1)S(1)} fusion(bf16[3072,1024]{1,0:T(8,128)(2,1)} %bitcast.121, bf16[3072,256]{1,0:T(8,128)(2,1)S(1)} %bitcast.130), kind=kOutput, calls=%fused_computation.39 | convolution fusion | flops 1610874880 | bytes 8388608 | tf_op jit(solution)/shard_map/dot_general | solution.py:127
  199.5 6.3 %psum.14 = f32[512]{0:T(512)S(1)} all-reduce(f32[512]{0:T(512)S(1)} %get-tuple-element.14), channel_id=1, replica_groups=mesh['groups'=2,'picks'=4,'heads'=4] {'heads'}, use_global_device_ids=true, to_apply=%region_7.8 | all-reduce | flops 512 | bytes 4096 | tf_op jit(solution)/shard_map/psum | solution.py:119
  209.2 2.0 copy-done.3
  212.2 5.9 %psum.15 = f32[1024]{0:T(1024)S(1)} all-reduce(f32[1024]{0:T(1024)S(1)} %fusion.32), channel_id=1, replica_groups=mesh['groups'=2,'picks'=4,'heads'=4] {'heads'}, use_global_device_ids=true, to_apply=%region_10.11 | all-reduce | flops 1024 | bytes 8192 | tf_op jit(solution)/shard_map/psum | solution.py:136
  218.4 3.3 %fusion.2 = f32[2,1024]{1,0:T(2,128)S(1)} fusion(f32[2,512]{1,0:T(2,128)S(1)} %bitcast.149, f32[1024]{0:T(1024)S(1)} %sub.53, f32[2,1024]{1,0:T(2,128)S(1)} %get-tuple-element.29, f32[2,1024,512]{1,2,0:T(8,128)} %copy-done.3), kind=kLoop, calls=%fused_computation.7 | loop fusion | flops 5240832 | bytes 4218880 | tf_op jit(solution)/shard_map/reduce_sum | solution.py:144
  223.7 3.1 %convolution_convert_fusion = bf16[3072,256]{1,0:T(8,128)(2,1)} fusion(bf16[3072,1024]{1,0:T(8,128)(2,1)S(1)} %bitcast.125, bf16[1024,256]{0,1:T(8,128)(2,1)S(1)} %bitcast.157), kind=kOutput, calls=%fused_computation.13 | convolution fusion | flops 1611399168 | bytes 8388608 | tf_op jit(solution)/shard_map/dot_general | solution.py:153
  226.8 36.4 %reduce-scatter.2.cloned.1.call-done = bf16[768,256]{1,0:T(8,128)(2,1)} async-done(((bf16[3072,256]{1,0:T(8,128)(2,1)}), bf16[768,256]{1,0:T(8,128)(2,1)}) %reduce-scatter.2.cloned.1.call-update) | async-done | bytes 393232 | tf_op jit(solution)/shard_map/reduce_scatter | solution.py:152
  (107 shorter events, 39.7 us)
Async XLA Ops:
  7.2 137.6 %copy-start = (bf16[3,1024,256]{2,1,0:T(8,128)(2,1)S(1)}, bf16[3,1024,256]{2,1,0:T(8,128)(2,1)}, u32[]{:S(2)}) copy-start(bf16[3,1024,256]{2,1,0:T(8,128)(2,1)} %param.19) | copy-start | bytes 4718596
  7.2 68.7 %all-gather.8.cloned.1.call-start = ((), (), s32[]{:S(2)}) async-start(), calls=%async_computation.1 | async-start | bytes 3932160 | tf_op jit(solution)/shard_map/all_gather | solution.py:63
  7.9 111.4 %all-gather.16.cloned.1.call-start = ((), (), s32[]{:S(2)}) async-start(), calls=%async_computation.6 | async-start | bytes 1310720 | tf_op jit(solution)/shard_map/all_gather | solution.py:77
  75.8 3.7 %copy-start.5 = (bf16[6,512,1024]{2,1,0:T(8,128)(2,1)S(1)}, bf16[6,512,1024]{2,1,0:T(8,128)(2,1)}, u32[]{:S(2)}) copy-start(bf16[6,512,1024]{2,1,0:T(8,128)(2,1)} %pad_maximum_fusion) | copy-start | bytes 18874372
  83.2 4.6 %copy-start.6 = (bf16[256,1024]{1,0:T(8,128)(2,1)S(1)}, bf16[256,1024]{1,0:T(8,128)(2,1)}, u32[]{:S(2)}) copy-start(bf16[256,1024]{1,0:T(8,128)(2,1)} %param.17) | copy-start | bytes 1572868
  83.2 6.3 %copy-start.9 = (f32[2,1024]{1,0:T(2,128)S(1)}, f32[2,1024]{1,0:T(2,128)}, u32[]{:S(2)}) copy-start(f32[2,1024]{1,0:T(2,128)} %param.18) | copy-start | bytes 24580
  87.7 53.5 %all-gather.10.cloned.1.call-start = ((), (), s32[]{:S(2)}) async-start(), calls=%async_computation.2 | async-start | bytes 1310720 | tf_op jit(solution)/shard_map/all_gather | solution.py:94
  87.8 13.1 %collective-permute-start = (bf16[256,1024]{1,0:T(8,128)(2,1)S(1)}, bf16[256,1024]{1,0:T(8,128)(2,1)S(1)}, u32[]{:S(2)}, u32[]{:S(2)}) collective-permute-start(bf16[256,1024]{1,0:T(8,128)(2,1)S(1)} %copy-done.6), channel_id=1, source_target_pairs={{0,3},{1,0},{2,1},{3,2},{4,7},{5,4},{6,5},{7,6},{8,11},{9,8},{10,9... | collective-permute-start | bytes 1572872 | tf_op jit(solution)/shard_map/ppermute | solution.py:30
  88.7 37.5 %collective-permute-start.1 = (bf16[256,1024]{1,0:T(8,128)(2,1)S(1)}, bf16[256,1024]{1,0:T(8,128)(2,1)S(1)}, u32[]{:S(2)}, u32[]{:S(2)}) collective-permute-start(bf16[256,1024]{1,0:T(8,128)(2,1)S(1)} %copy-done.6), channel_id=1, source_target_pairs={{0,2},{1,3},{2,0},{3,1},{4,6},{5,7},{6,4},{7,5},{8,10},{9,11},{10,... | collective-permute-start | bytes 1572872 | tf_op jit(solution)/shard_map/ppermute | solution.py:30
  89.4 37.7 %collective-permute-start.2 = (bf16[256,1024]{1,0:T(8,128)(2,1)S(1)}, bf16[256,1024]{1,0:T(8,128)(2,1)}, u32[]{:S(2)}, u32[]{:S(2)}) collective-permute-start(bf16[256,1024]{1,0:T(8,128)(2,1)S(1)} %copy-done.6), channel_id=1, source_target_pairs={{0,1},{1,2},{2,3},{3,0},{4,5},{5,6},{6,7},{7,4},{8,9},{9,10},{10,1... | collective-permute-start | bytes 1572872 | tf_op jit(solution)/shard_map/ppermute | solution.py:30
  126.1 61.6 %all-gather.12.cloned.1.call-start = ((), (), s32[]{:S(2)}) async-start(), calls=%async_computation.3 | async-start | bytes 1310720 | tf_op jit(solution)/shard_map/all_gather | solution.py:115
  146.5 4.7 %copy-start.10 = (s32[1024]{0:T(1024)S(1)}, s32[1024]{0:T(1024)}, u32[]{:S(2)}) copy-start(s32[1024]{0:T(1024)} %param.13) | copy-start | bytes 12292
  146.5 4.7 %copy-start.12 = (f32[64]{0:T(128)S(1)}, f32[64]{0:T(128)}, u32[]{:S(2)}) copy-start(f32[64]{0:T(128)} %param.14) | copy-start | bytes 772
  147.7 40.0 %copy-start.14 = (bf16[1024,256]{1,0:T(8,128)(2,1)S(1)}, bf16[1024,256]{1,0:T(8,128)(2,1)}, u32[]{:S(2)}) copy-start(bf16[1024,256]{1,0:T(8,128)(2,1)} %param.20) | copy-start | bytes 1572868
  147.8 58.6 %all-gather.14.cloned.1.call-start = ((), (), s32[]{:S(2)}) async-start(), calls=%async_computation.4 | async-start | bytes 1310720 | tf_op jit(solution)/shard_map/all_gather | solution.py:118
  147.8 12.9 %collective-permute-start.3 = (bf16[768,256]{1,0:T(8,128)(2,1)S(1)}, bf16[768,256]{1,0:T(8,128)(2,1)S(1)}, u32[]{:S(2)}, u32[]{:S(2)}) collective-permute-start(bf16[768,256]{1,0:T(8,128)(2,1)S(1)} %copy-done.7), channel_id=1, source_target_pairs={{0,12},{4,0},{8,4},{12,8},{1,13},{5,1},{9,5},{13,9},{2,14},{6,2},{... | collective-permute-start | bytes 1179656 | tf_op jit(solution)/shard_map/ppermute | solution.py:30
  151.3 34.0 %collective-permute-start.4 = (bf16[768,256]{1,0:T(8,128)(2,1)S(1)}, bf16[768,256]{1,0:T(8,128)(2,1)S(1)}, u32[]{:S(2)}, u32[]{:S(2)}) collective-permute-start(bf16[768,256]{1,0:T(8,128)(2,1)S(1)} %copy-done.7), channel_id=1, source_target_pairs={{0,8},{4,12},{8,0},{12,4},{1,9},{5,13},{9,1},{13,5},{2,10},{6,14},... | collective-permute-start | bytes 1179656 | tf_op jit(solution)/shard_map/ppermute | solution.py:30
  151.4 34.7 %collective-permute-start.5 = (bf16[768,256]{1,0:T(8,128)(2,1)S(1)}, bf16[768,256]{1,0:T(8,128)(2,1)S(1)}, u32[]{:S(2)}, u32[]{:S(2)}) collective-permute-start(bf16[768,256]{1,0:T(8,128)(2,1)S(1)} %copy-done.7), channel_id=1, source_target_pairs={{0,4},{4,8},{8,12},{12,0},{1,5},{5,9},{9,13},{13,1},{2,6},{6,10},{... | collective-permute-start | bytes 1179656 | tf_op jit(solution)/shard_map/ppermute | solution.py:30
  190.5 72.8 %reduce-scatter.2.cloned.1.call-start = ((), (), s32[]{:S(2)}) async-start(), calls=%async_computation.5 | async-start | bytes 1966080 | tf_op jit(solution)/shard_map/reduce_scatter | solution.py:152
  194.5 11.8 %copy-start.13 = (bf16[2,1024,256]{2,1,0:T(8,128)(2,1)S(1)}, bf16[2,1024,256]{2,1,0:T(8,128)(2,1)}, u32[]{:S(2)}) copy-start(bf16[2,1024,256]{2,1,0:T(8,128)(2,1)} %param.21) | copy-start | bytes 3145732
  205.8 5.4 %copy-start.11 = (f32[256]{0:T(256)S(1)}, f32[256]{0:T(256)}, u32[]{:S(2)}) copy-start(f32[256]{0:T(256)} %param.23) | copy-start | bytes 3076
  218.1 5.0 %copy-start.8 = (f32[1024]{0:T(1024)}, f32[1024]{0:T(1024)S(1)}, u32[]{:S(2)}) copy-start(f32[1024]{0:T(1024)S(1)} %psum.15) | copy-start | bytes 12292
  218.3 4.8 %slice-start = ((s8[6291456]{0:T(1024)(128)(4,1)}), s8[4194304]{0:T(1024)(128)(4,1)S(1)}, s32[]{:S(2)}) async-start(s8[6291456]{0:T(1024)(128)(4,1)} %bitcast.123), calls=%async_computation.7 | async-start | bytes 8388608
  223.1 42.1 %copy-start.1 = (bf16[3,1024,256]{2,1,0:T(8,128)(2,1)S(1)}, bf16[3,1024,256]{2,1,0:T(8,128)(2,1)}, u32[]{:S(2)}) copy-start(bf16[3,1024,256]{2,1,0:T(8,128)(2,1)} %param.19) | copy-start | bytes 4718596
  (6 other events, 12.7 us)
Sparse Core Ops, SparseCore 0:
  9.6 66.2 all-gather.7
  87.8 26.9 all-gather.15
  126.2 14.8 all-gather.9
  147.9 16.7 all-gather.11
  190.6 15.6 all-gather.13
  226.9 36.2 reduce-scatter.1
where the time goes:
time: 273 us; the launch traced here: 272 us
  waiting for transfers between devices  124 us (45%)
  other arithmetic  36.1 us (13%)
  matrix products  33.8 us (12%)
  local copies, waits for them, and re-layouts  31.4 us (12%)
  blocking collectives  25.6 us (9%)
  between operations  14.5 us (5%)
  starting transfers between devices  6.54 us (2%)
    ppermute x6, waiting for transfers between devices, ring_gather(): blocks.append(lax.ppermute(x, axis, [(i, (i - s) % n) for i in range(n)]))  41.8 us
    all_gather x1, waiting for transfers between devices, on_device(): piece = lax.all_gather(kv_weight, 'picks', axis=0, tiled=True)  39.9 us
    reduce_scatter x1, waiting for transfers between devices, on_device(): lax.psum_scatter(jnp.dot(enc.T, dquery, preferred_element_type=jnp.float3...  36.4 us
    another operation x1, other arithmetic  23.6 us
    unnamed x53, local copies, waits for them, and re-layouts  21.8 us
    all_gather x1, blocking collectives, on_device(): lax.all_gather(jnp.stack([top, total]), 'picks', axis=0, tiled=False)  13.3 us
    psum x1, blocking collectives, on_device(): power_two = lax.psum(jnp.sum(latents_out * latents_out, axis=1), 'heads')  6.34 us
    ppermute x6, starting transfers between devices, ring_gather(): blocks.append(lax.ppermute(x, axis, [(i, (i - s) % n) for i in range(n)]))  6.3 us
  transfers between devices with their start and end apart: 12, of which 7 were waited for; matrix products, arithmetic and copies ran while one was open for 24% of the time, Pallas kernels for 0%

commit v1 on v0

--- a/solution.py
+++ b/solution.py
@@ -60,7 +60,29 @@
     column = lax.axis_index("heads") * local
     enc = encode(coords)
     cross_full = ring_gather(cross_out, "heads", n_heads)
-    piece = lax.all_gather(kv_weight, "picks", axis=0, tiled=True)
+    e_now, work_now, side_arr = (
+        lax.axis_size("picks"),
+        lax.axis_index("picks"),
+        kv_weight.shape[0],
+    )
+    vals = [(dd, (dd + 1) % e_now) for dd in range(e_now)]
+    xs_all = [(dd, (dd - 1) % e_now) for dd in range(e_now)]
+    piece = jnp.zeros(
+        (*kv_weight.shape[:0], e_now * side_arr, *kv_weight.shape[1:]), kv_weight.dtype
+    )
+    piece = lax.dynamic_update_slice_in_dim(piece, kv_weight, work_now * side_arr, axis=0)
+    y = kept_arr = kv_weight
+    step_out = e_now // 2
+    for j0 in range(1, step_out + 1):
+        y = lax.ppermute(y, axis_name="picks", perm=vals)
+        piece = lax.dynamic_update_slice_in_dim(
+            piece, y, (work_now - j0) % e_now * side_arr, axis=0
+        )
+        if j0 < e_now - step_out:
+            kept_arr = lax.ppermute(kept_arr, axis_name="picks", perm=xs_all)
+            piece = lax.dynamic_update_slice_in_dim(
+                piece, kept_arr, (work_now + j0) % e_now * side_arr, axis=0
+            )
     keys_vals = jnp.dot(
         enc, piece.reshape(piece.shape[0], 2 * local), preferred_element_type=jnp.float32
     ).astype(jnp.bfloat16)

time: 273 us -> 262 us (0.960)
  waiting for transfers between devices: 124 us -> 97.7 us
  local copies, waits for them, and re-layouts: 31.4 us -> 38.2 us
  starting transfers between devices: 6.54 us -> 12 us
  other arithmetic: 36.1 us -> 39.7 us
    all_gather x1 -> x0, waiting for transfers between devices: 39.9 us -> none  [on_device(): piece = lax.all_gather(kv_weight, 'picks', axis=0, tiled=True)]
    ppermute x0 -> x3, waiting for transfers between devices: none -> 14 us  [the longest x2 14 us: on_device(): y = lax.ppermute(y, axis_name='picks', perm=vals)]
    dynamic_update_slice x0 -> x4, local copies, waits for them, and re-layouts: none -> 5.78 us  [the longest x2 3.45 us: on_device(): lax.dynamic_update_slice_in_dim(piece, y, (work_now - j0) % e_now * side_...]
    ppermute x0 -> x3, starting transfers between devices: none -> 5.23 us  [the longest x2 3.14 us: on_device(): y = lax.ppermute(y, axis_name='picks', perm=vals)]
    unnamed x53 -> x59, local copies, waits for them, and re-layouts: 21.8 us -> 20.9 us
  transfers between devices with their start and end apart: 12 -> 14, of which waited for: 7 -> 7; matrix products, arithmetic and copies ran while one was open for 24% -> 28% of each run, Pallas kernels for 0% -> 0%
where the time goes in v1:
time: 262 us; the launch traced here: 261 us
  waiting for transfers between devices  97.7 us (37%)
  other arithmetic  39.7 us (15%)
  local copies, waits for them, and re-layouts  38.2 us (15%)
  matrix products  33.6 us (13%)
  blocking collectives  25.3 us (10%)
  between operations  14.3 us (5%)
  starting transfers between devices  12 us (5%)
    ppermute x6, waiting for transfers between devices, ring_gather(): blocks.append(lax.ppermute(x, axis, [(i, (i - s) % n) for i in range(n)]))  40 us
    reduce_scatter x1, waiting for transfers between devices, on_device(): lax.psum_scatter(jnp.dot(enc.T, dquery, preferred_element_type=jnp.float3...  36.4 us
    another operation x1, other arithmetic  25.2 us
    unnamed x59, local copies, waits for them, and re-layouts  20.9 us
    ppermute x2, waiting for transfers between devices, on_device(): y = lax.ppermute(y, axis_name='picks', perm=vals)  14 us
    all_gather x1, blocking collectives, on_device(): lax.all_gather(jnp.stack([top, total]), 'picks', axis=0, tiled=False)  13.3 us
    all_gather x1, waiting for transfers between devices, on_device(): attended_full = lax.all_gather(attended, 'heads', axis=1, tiled=True)  6.73 us
    ppermute x6, starting transfers between devices, ring_gather(): blocks.append(lax.ppermute(x, axis, [(i, (i - s) % n) for i in range(n)]))  6.32 us
  transfers between devices with their start and end apart: 14, of which 7 were waited for; matrix products, arithmetic and copies ran while one was open for 28% of the time, Pallas kernels for 0%

profile of v1, /device:TPU:0, one launch (start us, length us, event | category | flops | bytes accessed | tf_op | source)
XLA Modules:
  0.0 260.8 jit_solution(16369146602328125392)
XLA Ops:
  7.2 3.1 %collective-permute-start = (bf16[768,2,256]{2,1,0:T(2,128)(2,1)}, bf16[768,2,256]{2,1,0:T(2,128)(2,1)}, u32[]{:S(2)}, u32[]{:S(2)}) collective-permute-start(bf16[768,2,256]{2,1,0:T(2,128)(2,1)} %param.16), channel_id=1, source_target_pairs={{0,4},{4,8},{8,12},{12,0},{1,5},{5,9},{9,13},{13,1},{2,6},{6,10},{... | collective-permute-start | bytes 2359304 | tf_op jit(solution)/shard_map/ppermute | solution.py:77
  10.3 2.1 collective-permute-start.1
  12.5 25.2 %fusion = (bf16[3,512,1024]{2,1,0:T(8,128)(2,1)}, bf16[3,512,1024]{2,1,0:T(8,128)(2,1)}) fusion(f32[3,1024]{1,0:T(4,128)} %param.12, f32[512]{0:T(512)S(1)} %maximum_multiply_fusion), kind=kLoop, calls=%fused_computation.2 | loop fusion | flops 4718592 | bytes 6305792 | tf_op jit(solution)/shard_map/convert
  41.4 5.1 %pad_maximum_fusion = bf16[6,512,1024]{2,1,0:T(8,128)(2,1)} fusion(bf16[3,512,1024]{2,1,0:T(8,128)(2,1)} %get-tuple-element.19, bf16[3,512,1024]{2,1,0:T(8,128)(2,1)S(1)} %copy-done.5), kind=kLoop, calls=%fused_computation.4 | loop fusion | flops 3145728 | bytes 12582912 | tf_op jit(solution)/shard_map/concatenate | solution.py:18
  50.0 14.0 %collective-permute-done.2 = bf16[768,2,256]{2,1,0:T(2,128)(2,1)} collective-permute-done((bf16[768,2,256]{2,1,0:T(2,128)(2,1)}, bf16[768,2,256]{2,1,0:T(2,128)(2,1)}, u32[]{:S(2)}, u32[]{:S(2)}) %collective-permute-start.2) | collective-permute-done | bytes 786464 | tf_op jit(solution)/shard_map/ppermute | solution.py:77
  66.2 2.2 copy-done.6
  68.4 3.5 %convolution_convert_fusion.1 = bf16[1024,512]{0,1:T(8,128)(2,1)S(1)} fusion(bf16[3072,1024]{1,0:T(8,128)(2,1)S(1)} %bitcast.123, bf16[3072,512]{1,0:T(8,128)(2,1)S(1)} %bitcast.127), kind=kOutput, calls=%fused_computation.33 | convolution fusion | flops 3221749760 | bytes 10485760 | tf_op jit(solution)/shard_map/dot_general | solution.py:86
  79.3 8.7 %collective-permute-done.3 = bf16[256,1024]{1,0:T(8,128)(2,1)S(1)} collective-permute-done((bf16[256,1024]{1,0:T(8,128)(2,1)S(1)}, bf16[256,1024]{1,0:T(8,128)(2,1)S(1)}, u32[]{:S(2)}, u32[]{:S(2)}) %collective-permute-start.3) | collective-permute-done | bytes 524320 | tf_op jit(solution)/shard_map/ppermute | solution.py:30
  88.8 3.1 %fusion.7 = f32[2,512]{1,0:T(2,128)S(1)} fusion(f32[2,512,1024]{2,1,0:T(8,128)} %copy-done.2, f32[2,512]{1,0:T(2,128)S(1)} %get-tuple-element.22), kind=kLoop, calls=%fused_computation.16 | loop fusion | flops 3144704 | bytes 4202496 | tf_op jit(solution)/shard_map/reduce_sum | solution.py:95
  91.9 13.3 %all-gather.1 = f32[8,2,512]{2,1,0:T(2,128)S(1)} all-gather(f32[2,2,512]{2,1,0:T(2,128)S(1)} %pad_maximum_fusion.1), channel_id=3, replica_groups=mesh['groups'=2,'picks'=4,'heads'=4] {'picks'}, dimensions={0}, use_global_device_ids=true | all-gather | bytes 40960 | tf_op jit(solution)/shard_map/all_gather | solution.py:100
  106.4 5.3 %fusion.44 = f32[512,2,1,128]{3,2,1,0:T(1,128)S(1)} fusion(f32[4,2,512,1]{0,3,1,2:T(1,128)} %copy.81, bf16[4,2,512,128]{3,2,1,0:T(8,128)(2,1)} %bitcast.156), kind=kOutput, calls=%fused_computation.51 | convolution fusion | flops 6291456 | bytes 1589248 | tf_op jit(solution)/shard_map/phl,phlc->hlc/dot_general | solution.py:104
  120.4 3.2 %constant_dynamic-slice_fusion.2 = bf16[4,256,1024]{2,1,0:T(8,128)(2,1)} fusion(bf16[8,256,1024]{2,1,0:T(8,128)(2,1)} %bitcast_dynamic-update-slice_fusion.1, s32[]{:T(128)S(6)} %select_n.63), kind=kLoop, calls=%fused_computation.88 | loop fusion | bytes 4194308 | tf_op jit(solution)/shard_map/jit(_roll_dynamic)/dynamic_slice | solution.py:32
  123.7 6.7 %all-gather.7.cloned.1.call-done = bf16[512,1024]{1,0:T(8,128)(2,1)} async-done(((bf16[512,256]{1,0:T(8,128)(2,1)}), bf16[512,1024]{1,0:T(8,128)(2,1)}) %all-gather.7.cloned.1.call-update) | async-done | bytes 1048592 | tf_op jit(solution)/shard_map/all_gather | solution.py:116
  130.4 3.3 %multiply_reduce_fusion.1 = (f32[512]{0:T(512)S(1)}, f32[512,1024]{1,0:T(8,128)S(1)}) fusion(bf16[512,1024]{1,0:T(8,128)(2,1)} %all-gather.7.cloned.1.call-done, bf16[1024,1024]{1,0:T(8,128)(2,1)} %bitcast.128, bf16[512,1024]{1,0:T(8,128)(2,1)S(1)} %copy-done.10), kind=kOutput, calls=%fused_computation.28 | convolution fusion | flops 1075838464 | bytes 6293504 | tf_op jit(solution)/shard_map/dot_general | solution.py:117
  136.9 3.4 %collective-permute-start.6 = (bf16[768,256]{1,0:T(8,128)(2,1)S(1)}, bf16[768,256]{1,0:T(8,128)(2,1)S(1)}, u32[]{:S(2)}, u32[]{:S(2)}) collective-permute-start(bf16[768,256]{1,0:T(8,128)(2,1)S(1)} %copy-done.8), channel_id=1, source_target_pairs={{0,12},{4,0},{8,4},{12,8},{1,13},{5,1},{9,5},{13,9},{2,14},{6,2},{... | collective-permute-start | bytes 1179656 | tf_op jit(solution)/shard_map/ppermute | solution.py:30
  142.3 7.5 %collective-permute-done.6 = bf16[768,256]{1,0:T(8,128)(2,1)S(1)} collective-permute-done((bf16[768,256]{1,0:T(8,128)(2,1)S(1)}, bf16[768,256]{1,0:T(8,128)(2,1)S(1)}, u32[]{:S(2)}, u32[]{:S(2)}) %collective-permute-start.6) | collective-permute-done | bytes 393248 | tf_op jit(solution)/shard_map/ppermute | solution.py:30
  150.6 23.8 %collective-permute-done.7 = bf16[768,256]{1,0:T(8,128)(2,1)S(1)} collective-permute-done((bf16[768,256]{1,0:T(8,128)(2,1)S(1)}, bf16[768,256]{1,0:T(8,128)(2,1)S(1)}, u32[]{:S(2)}, u32[]{:S(2)}) %collective-permute-start.7) | collective-permute-done | bytes 393248 | tf_op jit(solution)/shard_map/ppermute | solution.py:30
  176.8 2.7 %multiply_reduce_fusion.2 = (f32[512]{0:T(512)S(1)}, bf16[512,256]{1,0:T(8,128)(2,1)}, f32[512,256]{1,0:T(8,128)}) fusion(f32[256]{0:T(256)S(1)} %bitcast.155, bf16[512,1024]{0,1:T(8,128)(2,1)} %all-gather.9.cloned.1.call-done, bf16[1024,256]{1,0:T(8,128)(2,1)S(1)} %copy-done.17, f32[512,1024]{1,0:T(8,128)} %copy-done.18, s32[]{:T(128)S(6)} %select_n.54), kind=kOutput, calls=%fused_computation.61 | convolution fusion | flops 269090304 | bytes 2886660 | tf_op jit(solution)/shard_map/dot_general | solution.py:138
  183.7 5.0 %convolution_convert_fusion.3 = bf16[1024,256]{0,1:T(8,128)(2,1)S(1)} fusion(bf16[3072,1024]{1,0:T(8,128)(2,1)} %bitcast.122, bf16[3072,256]{1,0:T(8,128)(2,1)S(1)} %bitcast.130), kind=kOutput, calls=%fused_computation.39 | convolution fusion | flops 1610874880 | bytes 8388608 | tf_op jit(solution)/shard_map/dot_general | solution.py:149
  188.7 6.1 %psum.14 = f32[512]{0:T(512)S(1)} all-reduce(f32[512]{0:T(512)S(1)} %get-tuple-element.14), channel_id=1, replica_groups=mesh['groups'=2,'picks'=4,'heads'=4] {'heads'}, use_global_device_ids=true, to_apply=%region_7.8 | all-reduce | flops 512 | bytes 4096 | tf_op jit(solution)/shard_map/psum | solution.py:141
  201.3 5.9 %psum.15 = f32[1024]{0:T(1024)S(1)} all-reduce(f32[1024]{0:T(1024)S(1)} %fusion.32), channel_id=1, replica_groups=mesh['groups'=2,'picks'=4,'heads'=4] {'heads'}, use_global_device_ids=true, to_apply=%region_10.11 | all-reduce | flops 1024 | bytes 8192 | tf_op jit(solution)/shard_map/psum | solution.py:158
  207.4 3.3 %fusion.2 = f32[2,1024]{1,0:T(2,128)S(1)} fusion(f32[2,512]{1,0:T(2,128)S(1)} %bitcast.149, f32[1024]{0:T(1024)S(1)} %sub.61, f32[2,1024]{1,0:T(2,128)S(1)} %get-tuple-element.29, f32[2,1024,512]{1,2,0:T(8,128)} %copy-done.3), kind=kLoop, calls=%fused_computation.7 | loop fusion | flops 5240832 | bytes 4218880 | tf_op jit(solution)/shard_map/reduce_sum | solution.py:166
  212.8 3.1 %convolution_convert_fusion = bf16[3072,256]{1,0:T(8,128)(2,1)} fusion(bf16[3072,1024]{1,0:T(8,128)(2,1)S(1)} %bitcast.126, bf16[1024,256]{0,1:T(8,128)(2,1)S(1)} %bitcast.157), kind=kOutput, calls=%fused_computation.13 | convolution fusion | flops 1611399168 | bytes 8388608 | tf_op jit(solution)/shard_map/dot_general | solution.py:175
  215.9 36.4 %reduce-scatter.2.cloned.1.call-done = bf16[768,256]{1,0:T(8,128)(2,1)} async-done(((bf16[3072,256]{1,0:T(8,128)(2,1)}), bf16[768,256]{1,0:T(8,128)(2,1)}) %reduce-scatter.2.cloned.1.call-update) | async-done | bytes 393232 | tf_op jit(solution)/shard_map/reduce_scatter | solution.py:174
  (121 shorter events, 50.4 us)
Async XLA Ops:
  7.2 126.5 %copy-start = (bf16[3,1024,256]{2,1,0:T(8,128)(2,1)S(1)}, bf16[3,1024,256]{2,1,0:T(8,128)(2,1)}, u32[]{:S(2)}) copy-start(bf16[3,1024,256]{2,1,0:T(8,128)(2,1)} %param.19) | copy-start | bytes 4718596
  7.2 99.2 %all-gather.13.cloned.1.call-start = ((), (), s32[]{:S(2)}) async-start(), calls=%async_computation.5 | async-start | bytes 1310720 | tf_op jit(solution)/shard_map/all_gather | solution.py:99
  7.2 30.6 %collective-permute-start = (bf16[768,2,256]{2,1,0:T(2,128)(2,1)}, bf16[768,2,256]{2,1,0:T(2,128)(2,1)}, u32[]{:S(2)}, u32[]{:S(2)}) collective-permute-start(bf16[768,2,256]{2,1,0:T(2,128)(2,1)} %param.16), channel_id=1, source_target_pairs={{0,4},{4,8},{8,12},{12,0},{1,5},{5,9},{9,13},{13,1},{2,6},{6,10},{... | collective-permute-start | bytes 2359304 | tf_op jit(solution)/shard_map/ppermute | solution.py:77
  10.3 37.9 %collective-permute-start.1 = (bf16[768,2,256]{2,1,0:T(2,128)(2,1)}, bf16[768,2,256]{2,1,0:T(2,128)(2,1)}, u32[]{:S(2)}, u32[]{:S(2)}) collective-permute-start(bf16[768,2,256]{2,1,0:T(2,128)(2,1)} %param.16), channel_id=1, source_target_pairs={{0,12},{4,0},{8,4},{12,8},{1,13},{5,1},{9,5},{13,9},{2,14},{6,2},{... | collective-permute-start | bytes 2359304 | tf_op jit(solution)/shard_map/ppermute | solution.py:82
  37.8 26.1 %collective-permute-start.2 = (bf16[768,2,256]{2,1,0:T(2,128)(2,1)}, bf16[768,2,256]{2,1,0:T(2,128)(2,1)}, u32[]{:S(2)}, u32[]{:S(2)}) collective-permute-start(bf16[768,2,256]{2,1,0:T(2,128)(2,1)} %collective-permute-done), channel_id=1, source_target_pairs={{0,4},{4,8},{8,12},{12,0},{1,5},{5,9},{9,13},{13,1},{2,6},{6,10},{... | collective-permute-start | bytes 2359304 | tf_op jit(solution)/shard_map/ppermute | solution.py:77
  72.9 5.5 %copy-start.12 = (f32[2,1024]{1,0:T(2,128)S(1)}, f32[2,1024]{1,0:T(2,128)}, u32[]{:S(2)}) copy-start(f32[2,1024]{1,0:T(2,128)} %param.18) | copy-start | bytes 24580
  76.6 53.8 %all-gather.7.cloned.1.call-start = ((), (), s32[]{:S(2)}) async-start(), calls=%async_computation.1 | async-start | bytes 1310720 | tf_op jit(solution)/shard_map/all_gather | solution.py:116
  76.6 11.3 %collective-permute-start.3 = (bf16[256,1024]{1,0:T(8,128)(2,1)S(1)}, bf16[256,1024]{1,0:T(8,128)(2,1)S(1)}, u32[]{:S(2)}, u32[]{:S(2)}) collective-permute-start(bf16[256,1024]{1,0:T(8,128)(2,1)S(1)} %copy-done.7), channel_id=1, source_target_pairs={{0,3},{1,0},{2,1},{3,2},{4,7},{5,4},{6,5},{7,6},{8,11},{9,8},{10,9... | collective-permute-start | bytes 1572872 | tf_op jit(solution)/shard_map/ppermute | solution.py:30
  76.7 36.6 %collective-permute-start.4 = (bf16[256,1024]{1,0:T(8,128)(2,1)S(1)}, bf16[256,1024]{1,0:T(8,128)(2,1)S(1)}, u32[]{:S(2)}, u32[]{:S(2)}) collective-permute-start(bf16[256,1024]{1,0:T(8,128)(2,1)S(1)} %copy-done.7), channel_id=1, source_target_pairs={{0,2},{1,3},{2,0},{3,1},{4,6},{5,7},{6,4},{7,5},{8,10},{9,11},{10,... | collective-permute-start | bytes 1572872 | tf_op jit(solution)/shard_map/ppermute | solution.py:30
  78.2 35.9 %collective-permute-start.5 = (bf16[256,1024]{1,0:T(8,128)(2,1)S(1)}, bf16[256,1024]{1,0:T(8,128)(2,1)}, u32[]{:S(2)}, u32[]{:S(2)}) collective-permute-start(bf16[256,1024]{1,0:T(8,128)(2,1)S(1)} %copy-done.7), channel_id=1, source_target_pairs={{0,1},{1,2},{2,3},{3,0},{4,5},{5,6},{6,7},{7,4},{8,9},{9,10},{10,1... | collective-permute-start | bytes 1572872 | tf_op jit(solution)/shard_map/ppermute | solution.py:30
  113.2 63.6 %all-gather.9.cloned.1.call-start = ((), (), s32[]{:S(2)}) async-start(), calls=%async_computation.2 | async-start | bytes 1310720 | tf_op jit(solution)/shard_map/all_gather | solution.py:137
  117.7 12.7 %copy-start.10 = (bf16[512,1024]{1,0:T(8,128)(2,1)S(1)}, bf16[512,1024]{1,0:T(8,128)(2,1)}, u32[]{:S(2)}) copy-start(bf16[512,1024]{1,0:T(8,128)(2,1)} %param.15) | copy-start | bytes 3145732
  135.5 4.7 %copy-start.13 = (s32[1024]{0:T(1024)S(1)}, s32[1024]{0:T(1024)}, u32[]{:S(2)}) copy-start(s32[1024]{0:T(1024)} %param.13) | copy-start | bytes 12292
  135.5 4.7 %copy-start.15 = (f32[64]{0:T(128)S(1)}, f32[64]{0:T(128)}, u32[]{:S(2)}) copy-start(f32[64]{0:T(128)} %param.14) | copy-start | bytes 772
  136.8 40.0 %copy-start.17 = (bf16[1024,256]{1,0:T(8,128)(2,1)S(1)}, bf16[1024,256]{1,0:T(8,128)(2,1)}, u32[]{:S(2)}) copy-start(bf16[1024,256]{1,0:T(8,128)(2,1)} %param.20) | copy-start | bytes 1572868
  136.8 58.6 %all-gather.11.cloned.1.call-start = ((), (), s32[]{:S(2)}) async-start(), calls=%async_computation.3 | async-start | bytes 1310720 | tf_op jit(solution)/shard_map/all_gather | solution.py:140
  136.9 12.9 %collective-permute-start.6 = (bf16[768,256]{1,0:T(8,128)(2,1)S(1)}, bf16[768,256]{1,0:T(8,128)(2,1)S(1)}, u32[]{:S(2)}, u32[]{:S(2)}) collective-permute-start(bf16[768,256]{1,0:T(8,128)(2,1)S(1)} %copy-done.8), channel_id=1, source_target_pairs={{0,12},{4,0},{8,4},{12,8},{1,13},{5,1},{9,5},{13,9},{2,14},{6,2},{... | collective-permute-start | bytes 1179656 | tf_op jit(solution)/shard_map/ppermute | solution.py:30
  140.4 34.0 %collective-permute-start.7 = (bf16[768,256]{1,0:T(8,128)(2,1)S(1)}, bf16[768,256]{1,0:T(8,128)(2,1)S(1)}, u32[]{:S(2)}, u32[]{:S(2)}) collective-permute-start(bf16[768,256]{1,0:T(8,128)(2,1)S(1)} %copy-done.8), channel_id=1, source_target_pairs={{0,8},{4,12},{8,0},{12,4},{1,9},{5,13},{9,1},{13,5},{2,10},{6,14},... | collective-permute-start | bytes 1179656 | tf_op jit(solution)/shard_map/ppermute | solution.py:30
  140.5 34.7 %collective-permute-start.8 = (bf16[768,256]{1,0:T(8,128)(2,1)S(1)}, bf16[768,256]{1,0:T(8,128)(2,1)S(1)}, u32[]{:S(2)}, u32[]{:S(2)}) collective-permute-start(bf16[768,256]{1,0:T(8,128)(2,1)S(1)} %copy-done.8), channel_id=1, source_target_pairs={{0,4},{4,8},{8,12},{12,0},{1,5},{5,9},{9,13},{13,1},{2,6},{6,10},{... | collective-permute-start | bytes 1179656 | tf_op jit(solution)/shard_map/ppermute | solution.py:30
  179.5 72.8 %reduce-scatter.2.cloned.1.call-start = ((), (), s32[]{:S(2)}) async-start(), calls=%async_computation.4 | async-start | bytes 1966080 | tf_op jit(solution)/shard_map/reduce_scatter | solution.py:174
  183.7 11.7 %copy-start.16 = (bf16[2,1024,256]{2,1,0:T(8,128)(2,1)S(1)}, bf16[2,1024,256]{2,1,0:T(8,128)(2,1)}, u32[]{:S(2)}) copy-start(bf16[2,1024,256]{2,1,0:T(8,128)(2,1)} %param.21) | copy-start | bytes 3145732
  207.2 5.0 %copy-start.11 = (f32[1024]{0:T(1024)}, f32[1024]{0:T(1024)S(1)}, u32[]{:S(2)}) copy-start(f32[1024]{0:T(1024)S(1)} %psum.15) | copy-start | bytes 12292
  207.4 4.8 %slice-start = ((s8[6291456]{0:T(1024)(128)(4,1)}), s8[4194304]{0:T(1024)(128)(4,1)S(1)}, s32[]{:S(2)}) async-start(s8[6291456]{0:T(1024)(128)(4,1)} %bitcast.124), calls=%async_computation.6 | async-start | bytes 8388608
  212.7 41.5 %copy-start.1 = (bf16[3,1024,256]{2,1,0:T(8,128)(2,1)S(1)}, bf16[3,1024,256]{2,1,0:T(8,128)(2,1)}, u32[]{:S(2)}) copy-start(bf16[3,1024,256]{2,1,0:T(8,128)(2,1)} %param.19) | copy-start | bytes 4718596
  (11 other events, 27.1 us)
Sparse Core Ops, SparseCore 0:
  76.7 27.7 all-gather.12
  113.3 17.0 all-gather.6
  136.9 16.7 all-gather.8
  179.6 15.7 all-gather.10
  216.0 36.2 reduce-scatter.1
